TPU v7x, 32 devices: a whole 2x2x4 slice. The times are simulated.
32 devices in a mesh: row: 4 (over y, core), col: 8 (over z, x).
Axes of the slice: x: 2, y: 2, z: 4, core: 2. Of those that a mesh axis runs over, the one named last changes fastest.
Arguments:
- tokens: bfloat16 [1024, 16384], P('col', 'row'), may hold values from -6 to 6
- gate_weight: bfloat16 [16384, 26624], P('row', 'col'), may hold values from -0.046875 to 0.046875
- up_weight: bfloat16 [16384, 26624], P('row', 'col'), may hold values from -0.046875 to 0.046875
Outputs:
- hidden: bfloat16 [1024, 26624], P('row', 'col')
All inputs are finite; a program needn't handle non-finite values.
Results may differ from a plain program's by a relative error of at most 0.02.
Values may be sent and summed in bfloat16 or wider, within the bound.
No kernel may reach another device: no remote copies, remote signals or barrier semaphores. Data moves between devices by JAX's collectives and lax.ppermute only.
A program may use at most 192 MiB of HBM per device.

v0:
```python
import jax
import jax.numpy as jnp
from jax import lax
from jax.sharding import PartitionSpec as P


def on_device(tokens, gate_weight, up_weight):
    gathered = lax.all_gather(tokens, "col", axis=0, tiled=True)
    units = gate_weight.shape[1]
    gate_term = jnp.dot(gathered, gate_weight, preferred_element_type=jnp.float32)
    up_term = jnp.dot(gathered, up_weight, preferred_element_type=jnp.float32)
    summed = lax.psum_scatter(
        jnp.concatenate([gate_term, up_term], axis=1).astype(jnp.bfloat16),
        "row",
        scatter_dimension=0,
        tiled=True,
    ).astype(jnp.float32)
    gate = summed[:, :units]
    upper = summed[:, units:]
    return (jax.nn.silu(gate) * upper).astype(jnp.bfloat16)


def solution(mesh):
    placed = (P("col", "row"), P("row", "col"), P("row", "col"))
    return jax.shard_map(
        on_device, mesh=mesh, in_specs=placed, out_specs=P("row", "col"), check_vma=False
    )
```

profile of v0, /device:TPU:0, one launch (start us, length us, event | category | flops | bytes accessed | tf_op | source)
XLA Modules:
  0.0 333.6 jit_solution(17927107680310670530)
XLA Ops:
  6.5 0.0 all-gather.2.cloned.1.call-start
  6.5 0.7 all-gather.2.cloned.1.call-update
  7.3 0.0 reduce-scatter.2.cloned.1.call-start
  7.3 129.4 %all-gather.2.cloned.1.call-done = bf16[1024,4096]{1,0:T(8,128)(2,1)} async-done(((bf16[128,4096]{1,0:T(8,128)(2,1)}), bf16[1024,4096]{1,0:T(8,128)(2,1)}) %all-gather.2.cloned.1.call-update) | async-done | bytes 8388624 | tf_op jit(solution)/shard_map/all_gather | solution.py:8
  136.7 0.0 copy-start
  136.7 37.2 %convolution_convert_fusion = bf16[1024,3328]{1,0:T(8,128)(2,1)S(1)} fusion(bf16[1024,4096]{1,0:T(8,128)(2,1)} %all-gather.2.cloned.1.call-done, bf16[4096,3328]{1,0:T(8,128)(2,1)} %param.5), kind=kOutput, calls=%fused_computation.1 | convolution fusion | flops 27920695296 | bytes 42467328 | tf_op jit(solution)/shard_map/dot_general | solution.py:11
  173.9 0.0 copy-done
  173.9 33.8 %convolution_convert_fusion.1 = bf16[1024,3328]{1,0:T(8,128)(2,1)S(1)} fusion(bf16[1024,4096]{1,0:T(8,128)(2,1)S(1)} %copy-done, bf16[4096,3328]{1,0:T(8,128)(2,1)} %param.4), kind=kOutput, calls=%fused_computation.2 | convolution fusion | flops 27920695296 | bytes 42467328 | tf_op jit(solution)/shard_map/dot_general | solution.py:10
  207.7 9.0 %pad_maximum_fusion = bf16[1024,6656]{1,0:T(8,128)(2,1)} fusion(bf16[1024,3328]{1,0:T(8,128)(2,1)S(1)} %convolution_convert_fusion, bf16[1024,3328]{1,0:T(8,128)(2,1)S(1)} %convolution_convert_fusion.1), kind=kLoop, calls=%fused_computation | loop fusion | flops 27262976 | bytes 27262976 | tf_op jit(solution)/shard_map/concatenate | solution.py:13
  216.6 0.0 reduce-scatter.2.cloned.1.call-update
  216.6 105.1 %reduce-scatter.2.cloned.1.call-done = bf16[256,6656]{1,0:T(8,128)(2,1)} async-done(((bf16[1024,6656]{1,0:T(8,128)(2,1)}), bf16[256,6656]{1,0:T(8,128)(2,1)}) %reduce-scatter.2.cloned.1.call-update) | async-done | bytes 3407888 | tf_op jit(solution)/shard_map/reduce_scatter | solution.py:12
  321.8 2.7 convert_element_type.7
  324.5 2.2 fusion
Async XLA Ops:
  6.5 130.1 %all-gather.2.cloned.1.call-start = ((), (), s32[]{:S(2)}) async-start(), calls=%async_computation.1 | async-start | bytes 9437184 | tf_op jit(solution)/shard_map/all_gather | solution.py:8
  7.3 314.5 %reduce-scatter.2.cloned.1.call-start = ((), (), s32[]{:S(2)}) async-start(), calls=%async_computation.2 | async-start | bytes 17039360 | tf_op jit(solution)/shard_map/reduce_scatter | solution.py:12
  136.7 37.2 %copy-start = (bf16[1024,4096]{1,0:T(8,128)(2,1)S(1)}, bf16[1024,4096]{1,0:T(8,128)(2,1)}, u32[]{:S(2)}) copy-start(bf16[1024,4096]{1,0:T(8,128)(2,1)} %all-gather.2.cloned.1.call-done) | copy-start | bytes 25165828
Sparse Core Ops, SparseCore 0:
  9.5 127.1 all-gather.1
  216.8 104.9 reduce-scatter.1
where the time goes:
time: 334 us
  waiting for transfers between devices  235 us (70%)
  matrix products  70.9 us (21%)
  other arithmetic  13.9 us (4%)
  between operations  13.4 us (4%)
    all_gather x1, waiting for transfers between devices, on_device(): gathered = lax.all_gather(tokens, 'col', axis=0, tiled=True)  129 us
    reduce_scatter x1, waiting for transfers between devices, on_device(): lax.psum_scatter(jnp.concatenate([gate_term, up_term], axis=1).astype(jnp...  105 us
    dot_general x1, matrix products, on_device(): up_term = jnp.dot(gathered, up_weight, preferred_element_type=jnp.float32)  37.2 us
    dot_general x1, matrix products, on_device(): jnp.dot(gathered, gate_weight, preferred_element_type=jnp.float32)  33.8 us
    concatenate x1, other arithmetic, on_device(): jnp.concatenate([gate_term, up_term], axis=1).astype(jnp.bfloat16)  8.96 us
  transfers between devices with their start and end apart: 2, of which 2 were waited for; matrix products, arithmetic and copies ran while one was open for 0% of the time, Pallas kernels for 0%

commit v1 on v0

--- a/solution.py
+++ b/solution.py
@@ -4,8 +4,23 @@
 from jax.sharding import PartitionSpec as P
 
 
+def _enter_case(incoming_x, mesh_name):
+    workers = lax.axis_size(mesh_name)
+    pool = tuple(((rr, (rr + 1) % workers) for rr in range(workers)))
+    e_next, b_now = ([incoming_x], [incoming_x])
+    in_order = tuple(((rr, (rr - 1) % workers) for rr in range(workers)))
+    for _ in range(workers // 2):
+        e_next.append(lax.ppermute(e_next[-1], axis_name=mesh_name, perm=pool))
+    for _ in [*range((workers - 1) // 2)]:
+        far_arr = lax.ppermute(b_now[-1], axis_name=mesh_name, perm=in_order)
+        b_now.append(far_arr)
+    v_next = jnp.concatenate([*e_next[::-1], *b_now[1:]], axis=0)
+    arr_out = jnp.roll(v_next, (lax.axis_index(mesh_name) - workers // 2) * incoming_x.shape[0], 0)
+    return arr_out
+
+
 def on_device(tokens, gate_weight, up_weight):
-    gathered = lax.all_gather(tokens, "col", axis=0, tiled=True)
+    gathered = _enter_case(tokens, "col")
     units = gate_weight.shape[1]
     gate_term = jnp.dot(gathered, gate_weight, preferred_element_type=jnp.float32)
     up_term = jnp.dot(gathered, up_weight, preferred_element_type=jnp.float32)

time: 334 us -> 400 us (1.20)
  starting transfers between devices: 0.04 us -> 60.9 us
  local copies, waits for them, and re-layouts: 0.01 us -> 27.2 us
  waiting for transfers between devices: 235 us -> 212 us
    all_gather x1 -> x0, waiting for transfers between devices: 129 us -> none  [on_device(): gathered = lax.all_gather(tokens, 'col', axis=0, tiled=True)]
    ppermute x0 -> x7, waiting for transfers between devices: none -> 105 us  [the longest x4 105 us: _enter_case(): e_next.append(lax.ppermute(e_next[-1], axis_name=mesh_name, perm=pool))]
    ppermute x0 -> x7, starting transfers between devices: none -> 60.9 us  [the longest x3 52.9 us: _enter_case(): far_arr = lax.ppermute(b_now[-1], axis_name=mesh_name, perm=in_order)]
    unnamed x2 -> x21, local copies, waits for them, and re-layouts: 0.01 us -> 26.2 us
  transfers between devices with their start and end apart: 2 -> 8, of which waited for: 2 -> 5; matrix products, arithmetic and copies ran while one was open for 0% -> 3% of each run, Pallas kernels for 0% -> 0%
where the time goes in v1:
time: 400 us; the launch traced here: 399 us
  waiting for transfers between devices  212 us (53%)
  matrix products  72.3 us (18%)
  starting transfers between devices  60.9 us (15%)
  local copies, waits for them, and re-layouts  27.2 us (7%)
  other arithmetic  14 us (4%)
  between operations  13.4 us (3%)
    reduce_scatter x1, waiting for transfers between devices, on_device(): lax.psum_scatter(jnp.concatenate([gate_term, up_term], axis=1).astype(jnp...  106 us
    ppermute x4, waiting for transfers between devices, _enter_case(): e_next.append(lax.ppermute(e_next[-1], axis_name=mesh_name, perm=pool))  105 us
    ppermute x3, starting transfers between devices, _enter_case(): far_arr = lax.ppermute(b_now[-1], axis_name=mesh_name, perm=in_order)  52.9 us
    dot_general x1, matrix products, on_device(): jnp.dot(gathered, gate_weight, preferred_element_type=jnp.float32)  36.2 us
    dot_general x1, matrix products, on_device(): up_term = jnp.dot(gathered, up_weight, preferred_element_type=jnp.float32)  36.1 us
    unnamed x21, local copies, waits for them, and re-layouts  26.2 us
    concatenate x1, other arithmetic, on_device(): jnp.concatenate([gate_term, up_term], axis=1).astype(jnp.bfloat16)  8.99 us
    ppermute x4, starting transfers between devices, _enter_case(): e_next.append(lax.ppermute(e_next[-1], axis_name=mesh_name, perm=pool))  8.04 us
  transfers between devices with their start and end apart: 8, of which 5 were waited for; matrix products, arithmetic and copies ran while one was open for 3% of the time, Pallas kernels for 0%

profile of v1, /device:TPU:0, one launch (start us, length us, event | category | flops | bytes accessed | tf_op | source)
XLA Modules:
  0.0 399.4 jit_solution(13150401307096391865)
XLA Ops:
  6.5 3.0 collective-permute-start
  9.5 26.5 %collective-permute-done = bf16[128,4096]{1,0:T(8,128)(2,1)S(1)} collective-permute-done((bf16[128,4096]{1,0:T(8,128)(2,1)}, bf16[128,4096]{1,0:T(8,128)(2,1)S(1)}, u32[]{:S(2)}, u32[]{:S(2)}) %collective-permute-start) | collective-permute-done | bytes 1048608 | tf_op jit(solution)/shard_map/ppermute | solution.py:13
  36.0 4.7 %collective-permute-start.4 = (bf16[128,4096]{1,0:T(8,128)(2,1)}, bf16[128,4096]{1,0:T(8,128)(2,1)S(1)}, u32[]{:S(2)}, u32[]{:S(2)}) collective-permute-start(bf16[128,4096]{1,0:T(8,128)(2,1)} %param.3), channel_id=1, source_target_pairs={{0,7},{1,0},{2,1},{3,2},{4,3},{5,4},{6,5},{7,6},{8,15},{9,8},{10,9... | collective-permute-start | bytes 3145736 | tf_op jit(solution)/shard_map/ppermute | solution.py:15
  40.7 39.9 %collective-permute-done.1 = bf16[128,4096]{1,0:T(8,128)(2,1)S(1)} collective-permute-done((bf16[128,4096]{1,0:T(8,128)(2,1)S(1)}, bf16[128,4096]{1,0:T(8,128)(2,1)S(1)}, u32[]{:S(2)}, u32[]{:S(2)}) %collective-permute-start.1) | collective-permute-done | bytes 1048608 | tf_op jit(solution)/shard_map/ppermute | solution.py:13
  80.6 2.5 collective-permute-start.2
  83.1 23.5 %collective-permute-start.5 = (bf16[128,4096]{1,0:T(8,128)(2,1)S(1)}, bf16[128,4096]{1,0:T(8,128)(2,1)}, u32[]{:S(2)}, u32[]{:S(2)}) collective-permute-start(bf16[128,4096]{1,0:T(8,128)(2,1)S(1)} %collective-permute-done.4), channel_id=1, source_target_pairs={{0,7},{1,0},{2,1},{3,2},{4,3},{5,4},{6,5},{7,6},{8,15},{9,8},{10,9... | collective-permute-start | bytes 3145736 | tf_op jit(solution)/shard_map/ppermute | solution.py:15
  106.6 20.2 %collective-permute-done.2 = bf16[128,4096]{1,0:T(8,128)(2,1)} collective-permute-done((bf16[128,4096]{1,0:T(8,128)(2,1)S(1)}, bf16[128,4096]{1,0:T(8,128)(2,1)}, u32[]{:S(2)}, u32[]{:S(2)}) %collective-permute-start.2) | collective-permute-done | bytes 1048608 | tf_op jit(solution)/shard_map/ppermute | solution.py:13
  126.8 2.6 collective-permute-start.3
  129.4 24.6 %collective-permute-start.6 = (bf16[128,4096]{1,0:T(8,128)(2,1)}, bf16[128,4096]{1,0:T(8,128)(2,1)S(1)}, u32[]{:S(2)}, u32[]{:S(2)}) collective-permute-start(bf16[128,4096]{1,0:T(8,128)(2,1)} %collective-permute-done.5), channel_id=1, source_target_pairs={{0,7},{1,0},{2,1},{3,2},{4,3},{5,4},{6,5},{7,6},{8,15},{9,8},{10,9... | collective-permute-start | bytes 3145736 | tf_op jit(solution)/shard_map/ppermute | solution.py:15
  154.0 18.9 %collective-permute-done.3 = bf16[128,4096]{1,0:T(8,128)(2,1)} collective-permute-done((bf16[128,4096]{1,0:T(8,128)(2,1)}, bf16[128,4096]{1,0:T(8,128)(2,1)}, u32[]{:S(2)}, u32[]{:S(2)}) %collective-permute-start.3) | collective-permute-done | bytes 1048608 | tf_op jit(solution)/shard_map/ppermute | solution.py:13
  172.9 2.3 constant_dynamic-update-slice_fusion.15
  175.2 2.3 constant_dynamic-update-slice_fusion.14
  177.5 2.3 constant_dynamic-update-slice_fusion.13
  179.8 1.1 constant_dynamic-update-slice_fusion.12
  180.9 2.3 constant_dynamic-update-slice_fusion.11
  183.2 1.1 constant_dynamic-update-slice_fusion.10
  184.3 2.3 constant_dynamic-update-slice_fusion.9
  186.6 1.1 constant_dynamic-update-slice_fusion.8
  187.7 2.4 constant_dynamic-update-slice_fusion.7
  190.1 2.3 constant_dynamic-update-slice_fusion.6
  192.4 1.1 constant_dynamic-update-slice_fusion.5
  193.4 1.1 constant_dynamic-update-slice_fusion.4
  194.5 1.1 constant_dynamic-update-slice_fusion.3
  195.7 1.1 constant_dynamic-update-slice_fusion.2
  196.8 2.3 constant_dynamic-update-slice_fusion.1
  199.1 1.0 constant_dynamic-update-slice_fusion
  200.1 36.1 %convolution_convert_fusion = bf16[1024,3328]{1,0:T(8,128)(2,1)S(1)} fusion(bf16[4096,3328]{1,0:T(8,128)(2,1)} %param.5, bf16[2048,4096]{1,0:T(8,128)(2,1)} %constant_dynamic-update-slice_fusion, s32[]{:T(128)S(6)} %select_n.14), kind=kOutput, calls=%fused_computation.1 | convolution fusion | flops 27920695296 | bytes 42467332 | tf_op jit(solution)/shard_map/dot_general | solution.py:26
  236.3 36.2 %convolution_convert_fusion.1 = bf16[1024,3328]{1,0:T(8,128)(2,1)S(1)} fusion(bf16[4096,3328]{1,0:T(8,128)(2,1)} %param.4, bf16[2048,4096]{1,0:T(8,128)(2,1)} %constant_dynamic-update-slice_fusion, s32[]{:T(128)S(6)} %select_n.14), kind=kOutput, calls=%fused_computation.2 | convolution fusion | flops 27920695296 | bytes 42467332 | tf_op jit(solution)/shard_map/dot_general | solution.py:25
  272.4 9.0 %pad_maximum_fusion = bf16[1024,6656]{1,0:T(8,128)(2,1)} fusion(bf16[1024,3328]{1,0:T(8,128)(2,1)S(1)} %convolution_convert_fusion, bf16[1024,3328]{1,0:T(8,128)(2,1)S(1)} %convolution_convert_fusion.1), kind=kLoop, calls=%fused_computation | loop fusion | flops 27262976 | bytes 27262976 | tf_op jit(solution)/shard_map/concatenate | solution.py:28
  281.5 106.1 %reduce-scatter.2.cloned.1.call-done = bf16[256,6656]{1,0:T(8,128)(2,1)} async-done(((bf16[1024,6656]{1,0:T(8,128)(2,1)}), bf16[256,6656]{1,0:T(8,128)(2,1)}) %reduce-scatter.2.cloned.1.call-update) | async-done | bytes 3407888 | tf_op jit(solution)/shard_map/reduce_scatter | solution.py:27
  387.6 2.7 convert_element_type.7
  390.3 2.2 fusion.2
  (12 shorter events, 0.0 us)
Async XLA Ops:
  6.5 188.0 %copy-start = (bf16[128,4096]{1,0:T(8,128)(2,1)S(1)}, bf16[128,4096]{1,0:T(8,128)(2,1)}, u32[]{:S(2)}) copy-start(bf16[128,4096]{1,0:T(8,128)(2,1)} %param.3) | copy-start | bytes 3145732
  6.5 381.0 %reduce-scatter.2.cloned.1.call-start = ((), (), s32[]{:S(2)}) async-start(), calls=%async_computation.1 | async-start | bytes 17039360 | tf_op jit(solution)/shard_map/reduce_scatter | solution.py:27
  6.5 29.4 %collective-permute-start = (bf16[128,4096]{1,0:T(8,128)(2,1)}, bf16[128,4096]{1,0:T(8,128)(2,1)S(1)}, u32[]{:S(2)}, u32[]{:S(2)}) collective-permute-start(bf16[128,4096]{1,0:T(8,128)(2,1)} %param.3), channel_id=1, source_target_pairs={{0,1},{1,2},{2,3},{3,4},{4,5},{5,6},{6,7},{7,0},{8,9},{9,10},{10,1... | collective-permute-start | bytes 3145736 | tf_op jit(solution)/shard_map/ppermute | solution.py:13
  36.0 44.6 %collective-permute-start.1 = (bf16[128,4096]{1,0:T(8,128)(2,1)S(1)}, bf16[128,4096]{1,0:T(8,128)(2,1)S(1)}, u32[]{:S(2)}, u32[]{:S(2)}) collective-permute-start(bf16[128,4096]{1,0:T(8,128)(2,1)S(1)} %collective-permute-done), channel_id=1, source_target_pairs={{0,1},{1,2},{2,3},{3,4},{4,5},{5,6},{6,7},{7,0},{8,9},{9,10},{10,1... | collective-permute-start | bytes 3145736 | tf_op jit(solution)/shard_map/ppermute | solution.py:13
  36.0 47.1 %collective-permute-start.4 = (bf16[128,4096]{1,0:T(8,128)(2,1)}, bf16[128,4096]{1,0:T(8,128)(2,1)S(1)}, u32[]{:S(2)}, u32[]{:S(2)}) collective-permute-start(bf16[128,4096]{1,0:T(8,128)(2,1)} %param.3), channel_id=1, source_target_pairs={{0,7},{1,0},{2,1},{3,2},{4,3},{5,4},{6,5},{7,6},{8,15},{9,8},{10,9... | collective-permute-start | bytes 3145736 | tf_op jit(solution)/shard_map/ppermute | solution.py:15
  80.6 2.5 copy-start.1
  80.6 46.2 %collective-permute-start.2 = (bf16[128,4096]{1,0:T(8,128)(2,1)S(1)}, bf16[128,4096]{1,0:T(8,128)(2,1)}, u32[]{:S(2)}, u32[]{:S(2)}) collective-permute-start(bf16[128,4096]{1,0:T(8,128)(2,1)S(1)} %collective-permute-done.1), channel_id=1, source_target_pairs={{0,1},{1,2},{2,3},{3,4},{4,5},{5,6},{6,7},{7,0},{8,9},{9,10},{10,1... | collective-permute-start | bytes 3145736 | tf_op jit(solution)/shard_map/ppermute | solution.py:13
  83.1 46.3 %collective-permute-start.5 = (bf16[128,4096]{1,0:T(8,128)(2,1)S(1)}, bf16[128,4096]{1,0:T(8,128)(2,1)}, u32[]{:S(2)}, u32[]{:S(2)}) collective-permute-start(bf16[128,4096]{1,0:T(8,128)(2,1)S(1)} %collective-permute-done.4), channel_id=1, source_target_pairs={{0,7},{1,0},{2,1},{3,2},{4,3},{5,4},{6,5},{7,6},{8,15},{9,8},{10,9... | collective-permute-start | bytes 3145736 | tf_op jit(solution)/shard_map/ppermute | solution.py:15
  126.8 46.1 %collective-permute-start.3 = (bf16[128,4096]{1,0:T(8,128)(2,1)}, bf16[128,4096]{1,0:T(8,128)(2,1)}, u32[]{:S(2)}, u32[]{:S(2)}) collective-permute-start(bf16[128,4096]{1,0:T(8,128)(2,1)} %collective-permute-done.2), channel_id=1, source_target_pairs={{0,1},{1,2},{2,3},{3,4},{4,5},{5,6},{6,7},{7,0},{8,9},{9,10},{10,1... | collective-permute-start | bytes 3145736 | tf_op jit(solution)/shard_map/ppermute | solution.py:13
  129.4 63.0 %copy-start.2 = (bf16[128,4096]{1,0:T(8,128)(2,1)S(1)}, bf16[128,4096]{1,0:T(8,128)(2,1)}, u32[]{:S(2)}) copy-start(bf16[128,4096]{1,0:T(8,128)(2,1)} %copy-done.1) | copy-start | bytes 3145732
  129.4 57.2 %collective-permute-start.6 = (bf16[128,4096]{1,0:T(8,128)(2,1)}, bf16[128,4096]{1,0:T(8,128)(2,1)S(1)}, u32[]{:S(2)}, u32[]{:S(2)}) collective-permute-start(bf16[128,4096]{1,0:T(8,128)(2,1)} %collective-permute-done.5), channel_id=1, source_target_pairs={{0,7},{1,0},{2,1},{3,2},{4,3},{5,4},{6,5},{7,6},{8,15},{9,8},{10,9... | collective-permute-start | bytes 3145736 | tf_op jit(solution)/shard_map/ppermute | solution.py:15
Sparse Core Ops, SparseCore 0:
  281.6 105.9 reduce-scatter.1
